TPU v7x, 512 devices: a whole 4x8x8 slice. The times are simulated.
512 devices in a mesh: ctx: 64 (over y, x, core), head: 8 (over z).
Axes of the slice: x: 4, y: 8, z: 8, core: 2. Of those that a mesh axis runs over, the one named last changes fastest.
Arguments:
- tokens: bfloat16 [65536, 2048], P('ctx', 'head'), may hold values from -6 to 6
- w_qkv: bfloat16 [3, 2048, 2048], P(None, 'ctx', 'head'), may hold values from -0.125 to 0.125
- out_gain: float32 [2048], P('head'), may hold values from 0.25 to 1.75
- seg_ids: int32 [65536], P('ctx'), may hold values from 0 to 15, never falling along the last dimension, each value on 1 to 16384 neighbouring positions
Outputs:
- attended: bfloat16 [65536, 2048], P('ctx', 'head')
Inputs may be any that keep to these rules, and one draw needn't show every extreme that they name: `seg_ids`: segment numbers never fall along the stream; each segment covers 1 to 16384 consecutive tokens, and one covers exactly 16384.
All inputs are finite; a program needn't handle non-finite values.
Results may differ from a plain program's by a relative error of at most 0.012.
Values may be sent and summed in bfloat16 or wider, within the bound.
No kernel may reach another device: no remote copies, remote signals or barrier semaphores. Data moves between devices by JAX's collectives and lax.ppermute only.
A program may use at most 64 MiB of HBM per device.

v0:
```python
import jax
import jax.numpy as jnp
from jax import lax
from jax.sharding import PartitionSpec as P

HEAD_DIM = 128


def passed_along(value, axis, steps):
    count = lax.axis_size(axis)
    leading, last = (max(0, -steps), min(count, count - steps))
    return lax.ppermute(value, axis, [(source, source + steps) for source in range(leading, last)])


def feature_map(values):
    return (jax.nn.elu(values.astype(jnp.float32)) + 1.0).astype(jnp.bfloat16)


def combine(earlier, later):
    first_state, first_tail = earlier
    later_state, later_tail = later
    linked = (first_tail == later_tail) | (later_tail < 0.0)
    return (
        later_state + jnp.where(linked, first_state, 0.0),
        jnp.where(later_tail < 0.0, first_tail, later_tail),
    )


def prepare(projected, segment):
    row_count = segment.shape[0]
    head_count = projected.shape[2] // HEAD_DIM
    queries = feature_map(projected[0]).reshape(row_count, head_count, HEAD_DIM)
    key_map = feature_map(projected[1]).reshape(row_count, head_count, HEAD_DIM)
    values = projected[2].reshape(row_count, head_count, HEAD_DIM)
    seg_float = segment.astype(jnp.float32)
    tail_id = seg_float[-1]
    key_tail = jnp.where((seg_float == tail_id)[:, None, None], key_map, jnp.zeros_like(key_map))
    kv_state = jnp.einsum("thd,the->hde", key_tail, values, preferred_element_type=jnp.float32)
    return (queries, key_map, values, seg_float, kv_state, tail_id)


def complete(queries, key_map, values, seg_float, state_in, tail_in, out_gain):
    row_count, head_count = (queries.shape[0], queries.shape[1])
    state_low = state_in.astype(jnp.bfloat16)
    prefix = jnp.einsum("thd,hde->the", queries, state_low, preferred_element_type=jnp.float32)
    prefix = jnp.where((seg_float == tail_in)[:, None, None], prefix, 0.0)
    block_rows = min(512, row_count)
    positions = jnp.arange(row_count, dtype=jnp.int32)

    def one_block(blk_no):
        first_row = blk_no * block_rows
        query_blk = lax.dynamic_slice_in_dim(queries, first_row, block_rows, 0)
        query_pos = first_row + jnp.arange(block_rows, dtype=jnp.int32)
        query_seg = lax.dynamic_slice_in_dim(seg_float, first_row, block_rows, 0)
        scores = jnp.einsum("bhd,shd->hbs", query_blk, key_map, preferred_element_type=jnp.float32)
        visible = (positions[None, :] <= query_pos[:, None]) & (
            seg_float[None, :] == query_seg[:, None]
        )
        weights = jnp.where(visible[None], scores, 0.0).astype(jnp.bfloat16)
        return jnp.einsum("hbs,she->bhe", weights, values, preferred_element_type=jnp.float32)

    local_part = lax.map(one_block, jnp.arange(row_count // block_rows, dtype=jnp.int32))
    numerator = local_part.reshape(row_count, head_count, HEAD_DIM) + prefix
    inv_norm = lax.rsqrt(jnp.mean(numerator * numerator, axis=-1, keepdims=True) + 1e-05)
    result = numerator * inv_norm * out_gain.reshape(head_count, HEAD_DIM)
    return result.astype(jnp.bfloat16).reshape(row_count, head_count * HEAD_DIM)


def per_device(tokens, w_qkv, out_gain, seg_ids):
    whole = lax.all_gather(tokens, "head", axis=1, tiled=True)
    projected = jnp.einsum(
        "tr,grc->gtc",
        whole,
        lax.all_gather(w_qkv, "ctx", axis=1, tiled=True),
        preferred_element_type=jnp.float32,
    ).astype(jnp.bfloat16)
    queries, key_map, values, seg_float, kv_state, tail_id = prepare(projected, seg_ids)
    empty_state = jnp.zeros_like(kv_state)
    own_pair = (kv_state, tail_id)

    def hand_round(turn_no, carried):
        running, _ = carried
        incoming = (
            passed_along(running[0].astype(jnp.bfloat16), "ctx", 1).astype(jnp.float32),
            passed_along(running[1].astype(jnp.bfloat16), "ctx", 1).astype(jnp.float32),
        )
        return (combine(incoming, own_pair), incoming)

    start_pair = (empty_state, jnp.array(-1.0, jnp.float32))
    _, arrived = lax.fori_loop(0, lax.axis_size("ctx") - 1, hand_round, (own_pair, start_pair))
    state_in, tail_in = arrived
    return complete(queries, key_map, values, seg_float, state_in, tail_in, out_gain)


def solution(mesh):
    placed = (P("ctx", "head"), P(None, "ctx", "head"), P("head"), P("ctx"))
    return jax.shard_map(
        per_device, mesh=mesh, in_specs=placed, out_specs=P("ctx", "head"), check_vma=False
    )
```

profile of v0, /device:TPU:32, one launch (start us, length us, event | category | flops | bytes accessed | tf_op | source)
XLA Modules:
  0.0 1084.5 jit_solution(1804793181118891656)
XLA Ops:
  12.1 84.4 %all-gather.3.cloned.1.call-done = bf16[3,2048,256]{2,1,0:T(8,128)(2,1)} async-done(((bf16[3,32,256]{2,1,0:T(8,128)(2,1)}), bf16[3,2048,256]{2,1,0:T(8,128)(2,1)}) %all-gather.3.cloned.1.call-update) | async-done | bytes 3145744 | tf_op jit(solution)/shard_map/all_gather | solution.py:74
  96.5 67.6 %all-gather.5.cloned.1.call-done = bf16[1024,2048]{1,0:T(8,128)(2,1)} async-done(((bf16[1024,256]{1,0:T(8,128)(2,1)}), bf16[1024,2048]{1,0:T(8,128)(2,1)}) %all-gather.5.cloned.1.call-update) | async-done | bytes 4194320 | tf_op jit(solution)/shard_map/all_gather | solution.py:70
  164.0 6.6 fusion.15
  176.5 877.2 %while.28 = (s32[]{:T(128)}, bf16[2,128,128]{2,1,0:T(8,128)(2,1)S(1)}, bf16[]{:T(256)}, bf16[2,128,128]{2,1,0:T(8,128)(2,1)}, f32[]{:T(128)}, /*index=5*/f32[]{:...) while((s32[]{:T(128)}, bf16[2,128,128]{2,1,0:T(8,128)(2,1)S(1)}, bf16[]{:T(256)}, ...), condition=%wide.region_3.4_spmd, body=%wide.region_2.3_spmd.sunk | while | flops 163846 | bytes 590031 | solution.py:90
  195.3 5.4 collective-permute-done
  209.2 5.4 collective-permute-done
  223.1 5.4 collective-permute-done
  264.9 5.4 collective-permute-done
  278.8 5.4 collective-permute-done
  292.7 5.4 collective-permute-done
  306.6 5.4 collective-permute-done
  320.6 5.4 collective-permute-done
  334.5 5.4 collective-permute-done
  348.4 5.4 collective-permute-done
  362.3 5.4 collective-permute-done
  404.1 5.4 collective-permute-done
  418.0 5.4 collective-permute-done
  432.0 5.4 collective-permute-done
  445.9 5.4 collective-permute-done
  459.8 5.4 collective-permute-done
  473.7 5.4 collective-permute-done
  487.6 5.4 collective-permute-done
  529.4 5.4 collective-permute-done
  543.3 5.4 collective-permute-done
  557.3 5.4 collective-permute-done
  571.2 5.4 collective-permute-done
  585.1 5.4 collective-permute-done
  599.0 5.4 collective-permute-done
  613.0 5.4 collective-permute-done
  626.9 5.4 collective-permute-done
  668.6 5.4 collective-permute-done
  1056.0 19.2 %while.29 = (s32[]{:T(128)}, f32[2,512,2,128]{1,0,3,2:T(2,128)S(1)}, s32[2]{0:T(128)S(1)}, f32[1024]{0:T(1024)S(1)}, bf16[1024,2,128]{2,1,0:T(2,128)(2,1)S(1)}, ...) while((s32[]{:T(128)}, ...), condition=%wide.region_1.2_spmd.clone, body=%wide.region_0.1_spmd.clone.sunk | while | flops 540541440 | bytes 5519551 | solution.py:62
  (335 shorter events, 568.7 us)
Async XLA Ops:
  6.5 89.9 %all-gather.3.cloned.1.call-start = ((), (), s32[]{:S(2)}) async-start(), calls=%async_computation | async-start | bytes 3194880 | tf_op jit(solution)/shard_map/all_gather | solution.py:74
  7.3 156.8 %all-gather.5.cloned.1.call-start = ((), (), s32[]{:S(2)}) async-start(), calls=%async_computation.1 | async-start | bytes 4718592 | tf_op jit(solution)/shard_map/all_gather | solution.py:70
  176.5 13.3 %collective-permute-start.1 = (bf16[2,128,128]{2,1,0:T(8,128)(2,1)S(1)}, bf16[2,128,128]{2,1,0:T(8,128)(2,1)S(1)}, u32[]{:S(2)}, u32[]{:S(2)}) collective-permute-start(bf16[2,128,128]{2,1,0:T(8,128)(2,1)S(1)} %get-tuple-element.318), channel_id=1, source_target_pairs={{0,8},{8,16},{16,24},{24,32},{32,40},{40,48},{48,56},{56,64},{64,7... | collective-permute-start | bytes 196616 | tf_op jit(solution)/shard_map/while/body/eval_jaxpr/ppermute | solution.py:12
  190.5 13.3 %collective-permute-start.1 = (bf16[2,128,128]{2,1,0:T(8,128)(2,1)S(1)}, bf16[2,128,128]{2,1,0:T(8,128)(2,1)S(1)}, u32[]{:S(2)}, u32[]{:S(2)}) collective-permute-start(bf16[2,128,128]{2,1,0:T(8,128)(2,1)S(1)} %get-tuple-element.318), channel_id=1, source_target_pairs={{0,8},{8,16},{16,24},{24,32},{32,40},{40,48},{48,56},{56,64},{64,7... | collective-permute-start | bytes 196616 | tf_op jit(solution)/shard_map/while/body/eval_jaxpr/ppermute | solution.py:12
  204.4 13.3 %collective-permute-start.1 = (bf16[2,128,128]{2,1,0:T(8,128)(2,1)S(1)}, bf16[2,128,128]{2,1,0:T(8,128)(2,1)S(1)}, u32[]{:S(2)}, u32[]{:S(2)}) collective-permute-start(bf16[2,128,128]{2,1,0:T(8,128)(2,1)S(1)} %get-tuple-element.318), channel_id=1, source_target_pairs={{0,8},{8,16},{16,24},{24,32},{32,40},{40,48},{48,56},{56,64},{64,7... | collective-permute-start | bytes 196616 | tf_op jit(solution)/shard_map/while/body/eval_jaxpr/ppermute | solution.py:12
  218.3 13.3 %collective-permute-start.1 = (bf16[2,128,128]{2,1,0:T(8,128)(2,1)S(1)}, bf16[2,128,128]{2,1,0:T(8,128)(2,1)S(1)}, u32[]{:S(2)}, u32[]{:S(2)}) collective-permute-start(bf16[2,128,128]{2,1,0:T(8,128)(2,1)S(1)} %get-tuple-element.318), channel_id=1, source_target_pairs={{0,8},{8,16},{16,24},{24,32},{32,40},{40,48},{48,56},{56,64},{64,7... | collective-permute-start | bytes 196616 | tf_op jit(solution)/shard_map/while/body/eval_jaxpr/ppermute | solution.py:12
  287.9 13.3 %collective-permute-start.1 = (bf16[2,128,128]{2,1,0:T(8,128)(2,1)S(1)}, bf16[2,128,128]{2,1,0:T(8,128)(2,1)S(1)}, u32[]{:S(2)}, u32[]{:S(2)}) collective-permute-start(bf16[2,128,128]{2,1,0:T(8,128)(2,1)S(1)} %get-tuple-element.318), channel_id=1, source_target_pairs={{0,8},{8,16},{16,24},{24,32},{32,40},{40,48},{48,56},{56,64},{64,7... | collective-permute-start | bytes 196616 | tf_op jit(solution)/shard_map/while/body/eval_jaxpr/ppermute | solution.py:12
  301.9 13.3 %collective-permute-start.1 = (bf16[2,128,128]{2,1,0:T(8,128)(2,1)S(1)}, bf16[2,128,128]{2,1,0:T(8,128)(2,1)S(1)}, u32[]{:S(2)}, u32[]{:S(2)}) collective-permute-start(bf16[2,128,128]{2,1,0:T(8,128)(2,1)S(1)} %get-tuple-element.318), channel_id=1, source_target_pairs={{0,8},{8,16},{16,24},{24,32},{32,40},{40,48},{48,56},{56,64},{64,7... | collective-permute-start | bytes 196616 | tf_op jit(solution)/shard_map/while/body/eval_jaxpr/ppermute | solution.py:12
  315.8 13.3 %collective-permute-start.1 = (bf16[2,128,128]{2,1,0:T(8,128)(2,1)S(1)}, bf16[2,128,128]{2,1,0:T(8,128)(2,1)S(1)}, u32[]{:S(2)}, u32[]{:S(2)}) collective-permute-start(bf16[2,128,128]{2,1,0:T(8,128)(2,1)S(1)} %get-tuple-element.318), channel_id=1, source_target_pairs={{0,8},{8,16},{16,24},{24,32},{32,40},{40,48},{48,56},{56,64},{64,7... | collective-permute-start | bytes 196616 | tf_op jit(solution)/shard_map/while/body/eval_jaxpr/ppermute | solution.py:12
  329.7 13.3 %collective-permute-start.1 = (bf16[2,128,128]{2,1,0:T(8,128)(2,1)S(1)}, bf16[2,128,128]{2,1,0:T(8,128)(2,1)S(1)}, u32[]{:S(2)}, u32[]{:S(2)}) collective-permute-start(bf16[2,128,128]{2,1,0:T(8,128)(2,1)S(1)} %get-tuple-element.318), channel_id=1, source_target_pairs={{0,8},{8,16},{16,24},{24,32},{32,40},{40,48},{48,56},{56,64},{64,7... | collective-permute-start | bytes 196616 | tf_op jit(solution)/shard_map/while/body/eval_jaxpr/ppermute | solution.py:12
  343.6 13.3 %collective-permute-start.1 = (bf16[2,128,128]{2,1,0:T(8,128)(2,1)S(1)}, bf16[2,128,128]{2,1,0:T(8,128)(2,1)S(1)}, u32[]{:S(2)}, u32[]{:S(2)}) collective-permute-start(bf16[2,128,128]{2,1,0:T(8,128)(2,1)S(1)} %get-tuple-element.318), channel_id=1, source_target_pairs={{0,8},{8,16},{16,24},{24,32},{32,40},{40,48},{48,56},{56,64},{64,7... | collective-permute-start | bytes 196616 | tf_op jit(solution)/shard_map/while/body/eval_jaxpr/ppermute | solution.py:12
  413.3 13.3 %collective-permute-start.1 = (bf16[2,128,128]{2,1,0:T(8,128)(2,1)S(1)}, bf16[2,128,128]{2,1,0:T(8,128)(2,1)S(1)}, u32[]{:S(2)}, u32[]{:S(2)}) collective-permute-start(bf16[2,128,128]{2,1,0:T(8,128)(2,1)S(1)} %get-tuple-element.318), channel_id=1, source_target_pairs={{0,8},{8,16},{16,24},{24,32},{32,40},{40,48},{48,56},{56,64},{64,7... | collective-permute-start | bytes 196616 | tf_op jit(solution)/shard_map/while/body/eval_jaxpr/ppermute | solution.py:12
  427.2 13.3 %collective-permute-start.1 = (bf16[2,128,128]{2,1,0:T(8,128)(2,1)S(1)}, bf16[2,128,128]{2,1,0:T(8,128)(2,1)S(1)}, u32[]{:S(2)}, u32[]{:S(2)}) collective-permute-start(bf16[2,128,128]{2,1,0:T(8,128)(2,1)S(1)} %get-tuple-element.318), channel_id=1, source_target_pairs={{0,8},{8,16},{16,24},{24,32},{32,40},{40,48},{48,56},{56,64},{64,7... | collective-permute-start | bytes 196616 | tf_op jit(solution)/shard_map/while/body/eval_jaxpr/ppermute | solution.py:12
  441.1 13.3 %collective-permute-start.1 = (bf16[2,128,128]{2,1,0:T(8,128)(2,1)S(1)}, bf16[2,128,128]{2,1,0:T(8,128)(2,1)S(1)}, u32[]{:S(2)}, u32[]{:S(2)}) collective-permute-start(bf16[2,128,128]{2,1,0:T(8,128)(2,1)S(1)} %get-tuple-element.318), channel_id=1, source_target_pairs={{0,8},{8,16},{16,24},{24,32},{32,40},{40,48},{48,56},{56,64},{64,7... | collective-permute-start | bytes 196616 | tf_op jit(solution)/shard_map/while/body/eval_jaxpr/ppermute | solution.py:12
  455.0 13.3 %collective-permute-start.1 = (bf16[2,128,128]{2,1,0:T(8,128)(2,1)S(1)}, bf16[2,128,128]{2,1,0:T(8,128)(2,1)S(1)}, u32[]{:S(2)}, u32[]{:S(2)}) collective-permute-start(bf16[2,128,128]{2,1,0:T(8,128)(2,1)S(1)} %get-tuple-element.318), channel_id=1, source_target_pairs={{0,8},{8,16},{16,24},{24,32},{32,40},{40,48},{48,56},{56,64},{64,7... | collective-permute-start | bytes 196616 | tf_op jit(solution)/shard_map/while/body/eval_jaxpr/ppermute | solution.py:12
  468.9 13.3 %collective-permute-start.1 = (bf16[2,128,128]{2,1,0:T(8,128)(2,1)S(1)}, bf16[2,128,128]{2,1,0:T(8,128)(2,1)S(1)}, u32[]{:S(2)}, u32[]{:S(2)}) collective-permute-start(bf16[2,128,128]{2,1,0:T(8,128)(2,1)S(1)} %get-tuple-element.318), channel_id=1, source_target_pairs={{0,8},{8,16},{16,24},{24,32},{32,40},{40,48},{48,56},{56,64},{64,7... | collective-permute-start | bytes 196616 | tf_op jit(solution)/shard_map/while/body/eval_jaxpr/ppermute | solution.py:12
  482.9 13.3 %collective-permute-start.1 = (bf16[2,128,128]{2,1,0:T(8,128)(2,1)S(1)}, bf16[2,128,128]{2,1,0:T(8,128)(2,1)S(1)}, u32[]{:S(2)}, u32[]{:S(2)}) collective-permute-start(bf16[2,128,128]{2,1,0:T(8,128)(2,1)S(1)} %get-tuple-element.318), channel_id=1, source_target_pairs={{0,8},{8,16},{16,24},{24,32},{32,40},{40,48},{48,56},{56,64},{64,7... | collective-permute-start | bytes 196616 | tf_op jit(solution)/shard_map/while/body/eval_jaxpr/ppermute | solution.py:12
  552.5 13.3 %collective-permute-start.1 = (bf16[2,128,128]{2,1,0:T(8,128)(2,1)S(1)}, bf16[2,128,128]{2,1,0:T(8,128)(2,1)S(1)}, u32[]{:S(2)}, u32[]{:S(2)}) collective-permute-start(bf16[2,128,128]{2,1,0:T(8,128)(2,1)S(1)} %get-tuple-element.318), channel_id=1, source_target_pairs={{0,8},{8,16},{16,24},{24,32},{32,40},{40,48},{48,56},{56,64},{64,7... | collective-permute-start | bytes 196616 | tf_op jit(solution)/shard_map/while/body/eval_jaxpr/ppermute | solution.py:12
  566.4 13.3 %collective-permute-start.1 = (bf16[2,128,128]{2,1,0:T(8,128)(2,1)S(1)}, bf16[2,128,128]{2,1,0:T(8,128)(2,1)S(1)}, u32[]{:S(2)}, u32[]{:S(2)}) collective-permute-start(bf16[2,128,128]{2,1,0:T(8,128)(2,1)S(1)} %get-tuple-element.318), channel_id=1, source_target_pairs={{0,8},{8,16},{16,24},{24,32},{32,40},{40,48},{48,56},{56,64},{64,7... | collective-permute-start | bytes 196616 | tf_op jit(solution)/shard_map/while/body/eval_jaxpr/ppermute | solution.py:12
  580.3 13.3 %collective-permute-start.1 = (bf16[2,128,128]{2,1,0:T(8,128)(2,1)S(1)}, bf16[2,128,128]{2,1,0:T(8,128)(2,1)S(1)}, u32[]{:S(2)}, u32[]{:S(2)}) collective-permute-start(bf16[2,128,128]{2,1,0:T(8,128)(2,1)S(1)} %get-tuple-element.318), channel_id=1, source_target_pairs={{0,8},{8,16},{16,24},{24,32},{32,40},{40,48},{48,56},{56,64},{64,7... | collective-permute-start | bytes 196616 | tf_op jit(solution)/shard_map/while/body/eval_jaxpr/ppermute | solution.py:12
  594.3 13.3 %collective-permute-start.1 = (bf16[2,128,128]{2,1,0:T(8,128)(2,1)S(1)}, bf16[2,128,128]{2,1,0:T(8,128)(2,1)S(1)}, u32[]{:S(2)}, u32[]{:S(2)}) collective-permute-start(bf16[2,128,128]{2,1,0:T(8,128)(2,1)S(1)} %get-tuple-element.318), channel_id=1, source_target_pairs={{0,8},{8,16},{16,24},{24,32},{32,40},{40,48},{48,56},{56,64},{64,7... | collective-permute-start | bytes 196616 | tf_op jit(solution)/shard_map/while/body/eval_jaxpr/ppermute | solution.py:12
  608.2 13.3 %collective-permute-start.1 = (bf16[2,128,128]{2,1,0:T(8,128)(2,1)S(1)}, bf16[2,128,128]{2,1,0:T(8,128)(2,1)S(1)}, u32[]{:S(2)}, u32[]{:S(2)}) collective-permute-start(bf16[2,128,128]{2,1,0:T(8,128)(2,1)S(1)} %get-tuple-element.318), channel_id=1, source_target_pairs={{0,8},{8,16},{16,24},{24,32},{32,40},{40,48},{48,56},{56,64},{64,7... | collective-permute-start | bytes 196616 | tf_op jit(solution)/shard_map/while/body/eval_jaxpr/ppermute | solution.py:12
  677.8 13.3 %collective-permute-start.1 = (bf16[2,128,128]{2,1,0:T(8,128)(2,1)S(1)}, bf16[2,128,128]{2,1,0:T(8,128)(2,1)S(1)}, u32[]{:S(2)}, u32[]{:S(2)}) collective-permute-start(bf16[2,128,128]{2,1,0:T(8,128)(2,1)S(1)} %get-tuple-element.318), channel_id=1, source_target_pairs={{0,8},{8,16},{16,24},{24,32},{32,40},{40,48},{48,56},{56,64},{64,7... | collective-permute-start | bytes 196616 | tf_op jit(solution)/shard_map/while/body/eval_jaxpr/ppermute | solution.py:12
  691.7 13.3 %collective-permute-start.1 = (bf16[2,128,128]{2,1,0:T(8,128)(2,1)S(1)}, bf16[2,128,128]{2,1,0:T(8,128)(2,1)S(1)}, u32[]{:S(2)}, u32[]{:S(2)}) collective-permute-start(bf16[2,128,128]{2,1,0:T(8,128)(2,1)S(1)} %get-tuple-element.318), channel_id=1, source_target_pairs={{0,8},{8,16},{16,24},{24,32},{32,40},{40,48},{48,56},{56,64},{64,7... | collective-permute-start | bytes 196616 | tf_op jit(solution)/shard_map/while/body/eval_jaxpr/ppermute | solution.py:12
  705.6 13.3 %collective-permute-start.1 = (bf16[2,128,128]{2,1,0:T(8,128)(2,1)S(1)}, bf16[2,128,128]{2,1,0:T(8,128)(2,1)S(1)}, u32[]{:S(2)}, u32[]{:S(2)}) collective-permute-start(bf16[2,128,128]{2,1,0:T(8,128)(2,1)S(1)} %get-tuple-element.318), channel_id=1, source_target_pairs={{0,8},{8,16},{16,24},{24,32},{32,40},{40,48},{48,56},{56,64},{64,7... | collective-permute-start | bytes 196616 | tf_op jit(solution)/shard_map/while/body/eval_jaxpr/ppermute | solution.py:12
  719.6 13.3 %collective-permute-start.1 = (bf16[2,128,128]{2,1,0:T(8,128)(2,1)S(1)}, bf16[2,128,128]{2,1,0:T(8,128)(2,1)S(1)}, u32[]{:S(2)}, u32[]{:S(2)}) collective-permute-start(bf16[2,128,128]{2,1,0:T(8,128)(2,1)S(1)} %get-tuple-element.318), channel_id=1, source_target_pairs={{0,8},{8,16},{16,24},{24,32},{32,40},{40,48},{48,56},{56,64},{64,7... | collective-permute-start | bytes 196616 | tf_op jit(solution)/shard_map/while/body/eval_jaxpr/ppermute | solution.py:12
  733.5 13.3 %collective-permute-start.1 = (bf16[2,128,128]{2,1,0:T(8,128)(2,1)S(1)}, bf16[2,128,128]{2,1,0:T(8,128)(2,1)S(1)}, u32[]{:S(2)}, u32[]{:S(2)}) collective-permute-start(bf16[2,128,128]{2,1,0:T(8,128)(2,1)S(1)} %get-tuple-element.318), channel_id=1, source_target_pairs={{0,8},{8,16},{16,24},{24,32},{32,40},{40,48},{48,56},{56,64},{64,7... | collective-permute-start | bytes 196616 | tf_op jit(solution)/shard_map/while/body/eval_jaxpr/ppermute | solution.py:12
  747.4 13.3 %collective-permute-start.1 = (bf16[2,128,128]{2,1,0:T(8,128)(2,1)S(1)}, bf16[2,128,128]{2,1,0:T(8,128)(2,1)S(1)}, u32[]{:S(2)}, u32[]{:S(2)}) collective-permute-start(bf16[2,128,128]{2,1,0:T(8,128)(2,1)S(1)} %get-tuple-element.318), channel_id=1, source_target_pairs={{0,8},{8,16},{16,24},{24,32},{32,40},{40,48},{48,56},{56,64},{64,7... | collective-permute-start | bytes 196616 | tf_op jit(solution)/shard_map/while/body/eval_jaxpr/ppermute | solution.py:12
  817.0 13.3 %collective-permute-start.1 = (bf16[2,128,128]{2,1,0:T(8,128)(2,1)S(1)}, bf16[2,128,128]{2,1,0:T(8,128)(2,1)S(1)}, u32[]{:S(2)}, u32[]{:S(2)}) collective-permute-start(bf16[2,128,128]{2,1,0:T(8,128)(2,1)S(1)} %get-tuple-element.318), channel_id=1, source_target_pairs={{0,8},{8,16},{16,24},{24,32},{32,40},{40,48},{48,56},{56,64},{64,7... | collective-permute-start | bytes 196616 | tf_op jit(solution)/shard_map/while/body/eval_jaxpr/ppermute | solution.py:12
  830.9 13.3 %collective-permute-start.1 = (bf16[2,128,128]{2,1,0:T(8,128)(2,1)S(1)}, bf16[2,128,128]{2,1,0:T(8,128)(2,1)S(1)}, u32[]{:S(2)}, u32[]{:S(2)}) collective-permute-start(bf16[2,128,128]{2,1,0:T(8,128)(2,1)S(1)} %get-tuple-element.318), channel_id=1, source_target_pairs={{0,8},{8,16},{16,24},{24,32},{32,40},{40,48},{48,56},{56,64},{64,7... | collective-permute-start | bytes 196616 | tf_op jit(solution)/shard_map/while/body/eval_jaxpr/ppermute | solution.py:12
  844.9 13.3 %collective-permute-start.1 = (bf16[2,128,128]{2,1,0:T(8,128)(2,1)S(1)}, bf16[2,128,128]{2,1,0:T(8,128)(2,1)S(1)}, u32[]{:S(2)}, u32[]{:S(2)}) collective-permute-start(bf16[2,128,128]{2,1,0:T(8,128)(2,1)S(1)} %get-tuple-element.318), channel_id=1, source_target_pairs={{0,8},{8,16},{16,24},{24,32},{32,40},{40,48},{48,56},{56,64},{64,7... | collective-permute-start | bytes 196616 | tf_op jit(solution)/shard_map/while/body/eval_jaxpr/ppermute | solution.py:12
  858.8 13.3 %collective-permute-start.1 = (bf16[2,128,128]{2,1,0:T(8,128)(2,1)S(1)}, bf16[2,128,128]{2,1,0:T(8,128)(2,1)S(1)}, u32[]{:S(2)}, u32[]{:S(2)}) collective-permute-start(bf16[2,128,128]{2,1,0:T(8,128)(2,1)S(1)} %get-tuple-element.318), channel_id=1, source_target_pairs={{0,8},{8,16},{16,24},{24,32},{32,40},{40,48},{48,56},{56,64},{64,7... | collective-permute-start | bytes 196616 | tf_op jit(solution)/shard_map/while/body/eval_jaxpr/ppermute | solution.py:12
  (100 other events, 2743.7 us)
Sparse Core Ops, SparseCore 0:
  10.8 85.6 all-gather.2
  98.5 65.5 all-gather.4
where the time goes:
time: 1090 us; the launch traced here: 1080 us
  waiting for transfers between devices  494 us (45%)
  starting transfers between devices  302 us (28%)
  loops' own time  196 us (18%)
  other arithmetic  50.1 us (5%)
  local copies, waits for them, and re-layouts  16.1 us (1%)
  between operations  14.9 us (1%)
  matrix products  11.9 us (1%)
    ppermute x126, waiting for transfers between devices, passed_along(): lax.ppermute(value, axis, [(source, source + steps) for source in range(l...  340 us
    ppermute x126, starting transfers between devices, passed_along(): lax.ppermute(value, axis, [(source, source + steps) for source in range(l...  302 us
    another operation x1, loops' own time, per_device(): lax.fori_loop(0, lax.axis_size('ctx') - 1, hand_round, (own_pair, start_p...  194 us
    all_gather x1, waiting for transfers between devices, per_device(): lax.all_gather(w_qkv, 'ctx', axis=1, tiled=True)  84.4 us
    all_gather x1, waiting for transfers between devices, per_device(): whole = lax.all_gather(tokens, 'head', axis=1, tiled=True)  67.6 us
    add x63, other arithmetic, combine(): later_state + jnp.where(linked, first_state, 0.0)  40.5 us
  transfers between devices with their start and end apart: 128, of which 65 were waited for; matrix products, arithmetic and copies ran while one was open for 0% of the time, Pallas kernels for 0%

commit v1 on v0

--- a/solution.py
+++ b/solution.py
@@ -67,7 +67,16 @@
 
 
 def per_device(tokens, w_qkv, out_gain, seg_ids):
-    whole = lax.all_gather(tokens, "head", axis=1, tiled=True)
+    ways = lax.axis_size("head")
+    up = [(d, (d + 1) % ways) for d in range(ways)]
+    down = [(d, (d - 1) % ways) for d in range(ways)]
+    earlier_2, later_2 = ([tokens], [tokens])
+    for _ in range(ways // 2):
+        earlier_2.append(lax.ppermute(earlier_2[-1], "head", up))
+    for _ in range((ways - 1) // 2):
+        later_2.append(lax.ppermute(later_2[-1], "head", down))
+    line = jnp.concatenate([*earlier_2[::-1], *later_2[1:]], axis=1)
+    whole = jnp.roll(line, (lax.axis_index("head") - ways // 2) * tokens.shape[1], axis=1)
     projected = jnp.einsum(
         "tr,grc->gtc",
         whole,

time: 1090 us -> 1020 us (0.936)
  waiting for transfers between devices: 494 us -> 385 us
  starting transfers between devices: 302 us -> 326 us
  local copies, waits for them, and re-layouts: 16.1 us -> 34 us
    all_gather x1, waiting for transfers between devices: 84.4 us -> 2.85 us  [per_device(): lax.all_gather(w_qkv, 'ctx', axis=1, tiled=True)]
    all_gather x1 -> x0, waiting for transfers between devices: 67.6 us -> none  [per_device(): whole = lax.all_gather(tokens, 'head', axis=1, tiled=True)]
    ppermute x0 -> x7, waiting for transfers between devices: none -> 39.9 us  [the longest x4 39.9 us: per_device(): earlier_2.append(lax.ppermute(earlier_2[-1], 'head', up))]
    ppermute x0 -> x7, starting transfers between devices: none -> 25.4 us  [the longest x3 15.4 us: per_device(): later_2.append(lax.ppermute(later_2[-1], 'head', down))]
    unnamed x9 -> x26, local copies, waits for them, and re-layouts: 0.31 us -> 17.4 us
  transfers between devices with their start and end apart: 128 -> 134, of which waited for: 65 -> 68; matrix products, arithmetic and copies ran while one was open for 0% -> 2% of each run, Pallas kernels for 0% -> 0%
where the time goes in v1:
time: 1020 us; the launch traced here: 1010 us
  waiting for transfers between devices  385 us (38%)
  starting transfers between devices  326 us (32%)
  loops' own time  189 us (19%)
  other arithmetic  49.3 us (5%)
  local copies, waits for them, and re-layouts  34 us (3%)
  between operations  14.8 us (1%)
  matrix products  12.3 us (1%)
    ppermute x126, waiting for transfers between devices, passed_along(): lax.ppermute(value, axis, [(source, source + steps) for source in range(l...  342 us
    ppermute x126, starting transfers between devices, passed_along(): lax.ppermute(value, axis, [(source, source + steps) for source in range(l...  301 us
    another operation x1, loops' own time, per_device(): lax.fori_loop(0, lax.axis_size('ctx') - 1, hand_round, (own_pair, start_p...  188 us
    ppermute x4, waiting for transfers between devices, per_device(): earlier_2.append(lax.ppermute(earlier_2[-1], 'head', up))  39.9 us
    add x63, other arithmetic, combine(): later_state + jnp.where(linked, first_state, 0.0)  39.8 us
  transfers between devices with their start and end apart: 134, of which 68 were waited for; matrix products, arithmetic and copies ran while one was open for 2% of the time, Pallas kernels for 0%

profile of v1, /device:TPU:32, one launch (start us, length us, event | category | flops | bytes accessed | tf_op | source)
XLA Modules:
  0.0 1010.8 jit_solution(15903880386415833679)
XLA Ops:
  11.5 18.8 %collective-permute-done.2 = bf16[1024,256]{1,0:T(8,128)(2,1)S(1)} collective-permute-done((bf16[1024,256]{1,0:T(8,128)(2,1)}, bf16[1024,256]{1,0:T(8,128)(2,1)S(1)}, u32[]{:S(2)}, u32[]{:S(2)}) %collective-permute-start.2) | collective-permute-done | bytes 524320 | tf_op jit(solution)/shard_map/ppermute | solution.py:75
  37.4 9.1 collective-permute-done.3
  53.6 8.2 collective-permute-done.4
  96.4 6.6 fusion.16
  109.6 870.3 %while.28 = (s32[]{:T(128)}, bf16[2,128,128]{2,1,0:T(8,128)(2,1)S(1)}, bf16[]{:T(256)}, bf16[2,128,128]{2,1,0:T(8,128)(2,1)}, f32[]{:T(128)}, /*index=5*/f32[]{:...) while((s32[]{:T(128)}, bf16[2,128,128]{2,1,0:T(8,128)(2,1)S(1)}, bf16[]{:T(256)}, ...), condition=%wide.region_3.4_spmd, body=%wide.region_2.3_spmd.sunk | while | flops 163846 | bytes 590031 | solution.py:99
  114.7 5.4 collective-permute-done
  128.5 5.4 collective-permute-done
  142.3 5.4 collective-permute-done
  156.1 5.4 collective-permute-done
  183.8 5.4 collective-permute-done
  197.6 5.4 collective-permute-done
  225.2 5.4 collective-permute-done
  239.0 5.4 collective-permute-done
  266.6 5.4 collective-permute-done
  280.4 5.4 collective-permute-done
  308.0 5.4 collective-permute-done
  321.8 5.4 collective-permute-done
  335.7 5.4 collective-permute-done
  349.5 5.4 collective-permute-done
  363.3 5.4 collective-permute-done
  377.1 5.4 collective-permute-done
  390.9 5.4 collective-permute-done
  404.7 5.4 collective-permute-done
  418.5 5.4 collective-permute-done
  446.1 5.4 collective-permute-done
  459.9 5.4 collective-permute-done
  487.6 5.4 collective-permute-done
  501.4 5.4 collective-permute-done
  529.0 5.4 collective-permute-done
  542.8 5.4 collective-permute-done
  570.4 5.4 collective-permute-done
  982.2 19.3 %while.29 = (s32[]{:T(128)}, f32[2,512,2,128]{1,0,3,2:T(2,128)S(1)}, s32[2]{0:T(128)S(1)}, f32[1024]{0:T(1024)S(1)}, bf16[1024,2,128]{2,1,0:T(2,128)(2,1)S(1)}, ...) while((s32[]{:T(128)}, ...), condition=%wide.region_1.2_spmd.clone, body=%wide.region_0.1_spmd.clone.sunk | while | flops 540541440 | bytes 5519543 | solution.py:62
  (364 shorter events, 623.1 us)
Async XLA Ops:
  6.5 89.9 %all-gather.2.cloned.1.call-start = ((), (), s32[]{:S(2)}) async-start(), calls=%async_computation | async-start | bytes 3194880 | tf_op jit(solution)/shard_map/all_gather | solution.py:83
  7.3 23.1 %collective-permute-start.2 = (bf16[1024,256]{1,0:T(8,128)(2,1)}, bf16[1024,256]{1,0:T(8,128)(2,1)S(1)}, u32[]{:S(2)}, u32[]{:S(2)}) collective-permute-start(bf16[1024,256]{1,0:T(8,128)(2,1)} %param.8), channel_id=1, source_target_pairs={{0,1},{1,2},{2,3},{3,4},{4,5},{5,6},{6,7},{7,0},{8,9},{9,10},{10,1... | collective-permute-start | bytes 1572872 | tf_op jit(solution)/shard_map/ppermute | solution.py:75
  30.3 16.2 %collective-permute-start.3 = (bf16[1024,256]{1,0:T(8,128)(2,1)S(1)}, bf16[1024,256]{1,0:T(8,128)(2,1)S(1)}, u32[]{:S(2)}, u32[]{:S(2)}) collective-permute-start(bf16[1024,256]{1,0:T(8,128)(2,1)S(1)} %collective-permute-done.2), channel_id=1, source_target_pairs={{0,1},{1,2},{2,3},{3,4},{4,5},{5,6},{6,7},{7,0},{8,9},{9,10},{10,1... | collective-permute-start | bytes 1572872 | tf_op jit(solution)/shard_map/ppermute | solution.py:75
  32.3 16.2 %collective-permute-start.6 = (bf16[1024,256]{1,0:T(8,128)(2,1)}, bf16[1024,256]{1,0:T(8,128)(2,1)S(1)}, u32[]{:S(2)}, u32[]{:S(2)}) collective-permute-start(bf16[1024,256]{1,0:T(8,128)(2,1)} %param.8), channel_id=1, source_target_pairs={{0,7},{1,0},{2,1},{3,2},{4,3},{5,4},{6,5},{7,6},{8,15},{9,8},{10,9... | collective-permute-start | bytes 1572872 | tf_op jit(solution)/shard_map/ppermute | solution.py:77
  46.5 15.3 %collective-permute-start.4 = (bf16[1024,256]{1,0:T(8,128)(2,1)S(1)}, bf16[1024,256]{1,0:T(8,128)(2,1)S(1)}, u32[]{:S(2)}, u32[]{:S(2)}) collective-permute-start(bf16[1024,256]{1,0:T(8,128)(2,1)S(1)} %collective-permute-done.3), channel_id=1, source_target_pairs={{0,1},{1,2},{2,3},{3,4},{4,5},{5,6},{6,7},{7,0},{8,9},{9,10},{10,1... | collective-permute-start | bytes 1572872 | tf_op jit(solution)/shard_map/ppermute | solution.py:75
  48.5 18.9 %collective-permute-start.7 = (bf16[1024,256]{1,0:T(8,128)(2,1)S(1)}, bf16[1024,256]{1,0:T(8,128)(2,1)S(1)}, u32[]{:S(2)}, u32[]{:S(2)}) collective-permute-start(bf16[1024,256]{1,0:T(8,128)(2,1)S(1)} %collective-permute-done.6), channel_id=1, source_target_pairs={{0,7},{1,0},{2,1},{3,2},{4,3},{5,4},{6,5},{7,6},{8,15},{9,8},{10,9... | collective-permute-start | bytes 1572872 | tf_op jit(solution)/shard_map/ppermute | solution.py:77
  61.8 14.5 %collective-permute-start.5 = (bf16[1024,256]{1,0:T(8,128)(2,1)S(1)}, bf16[1024,256]{1,0:T(8,128)(2,1)}, u32[]{:S(2)}, u32[]{:S(2)}) collective-permute-start(bf16[1024,256]{1,0:T(8,128)(2,1)S(1)} %collective-permute-done.4), channel_id=1, source_target_pairs={{0,1},{1,2},{2,3},{3,4},{4,5},{5,6},{6,7},{7,0},{8,9},{9,10},{10,1... | collective-permute-start | bytes 1572872 | tf_op jit(solution)/shard_map/ppermute | solution.py:75
  67.4 17.2 %collective-permute-start.8 = (bf16[1024,256]{1,0:T(8,128)(2,1)S(1)}, bf16[1024,256]{1,0:T(8,128)(2,1)S(1)}, u32[]{:S(2)}, u32[]{:S(2)}) collective-permute-start(bf16[1024,256]{1,0:T(8,128)(2,1)S(1)} %collective-permute-done.7), channel_id=1, source_target_pairs={{0,7},{1,0},{2,1},{3,2},{4,3},{5,4},{6,5},{7,6},{8,15},{9,8},{10,9... | collective-permute-start | bytes 1572872 | tf_op jit(solution)/shard_map/ppermute | solution.py:77
  109.7 13.4 %collective-permute-start.1 = (bf16[2,128,128]{2,1,0:T(8,128)(2,1)S(1)}, bf16[2,128,128]{2,1,0:T(8,128)(2,1)S(1)}, u32[]{:S(2)}, u32[]{:S(2)}) collective-permute-start(bf16[2,128,128]{2,1,0:T(8,128)(2,1)S(1)} %get-tuple-element.318), channel_id=1, source_target_pairs={{0,8},{8,16},{16,24},{24,32},{32,40},{40,48},{48,56},{56,64},{64,7... | collective-permute-start | bytes 196616 | tf_op jit(solution)/shard_map/while/body/eval_jaxpr/ppermute | solution.py:12
  137.5 13.2 %collective-permute-start.1 = (bf16[2,128,128]{2,1,0:T(8,128)(2,1)S(1)}, bf16[2,128,128]{2,1,0:T(8,128)(2,1)S(1)}, u32[]{:S(2)}, u32[]{:S(2)}) collective-permute-start(bf16[2,128,128]{2,1,0:T(8,128)(2,1)S(1)} %get-tuple-element.318), channel_id=1, source_target_pairs={{0,8},{8,16},{16,24},{24,32},{32,40},{40,48},{48,56},{56,64},{64,7... | collective-permute-start | bytes 196616 | tf_op jit(solution)/shard_map/while/body/eval_jaxpr/ppermute | solution.py:12
  179.0 13.2 %collective-permute-start.1 = (bf16[2,128,128]{2,1,0:T(8,128)(2,1)S(1)}, bf16[2,128,128]{2,1,0:T(8,128)(2,1)S(1)}, u32[]{:S(2)}, u32[]{:S(2)}) collective-permute-start(bf16[2,128,128]{2,1,0:T(8,128)(2,1)S(1)} %get-tuple-element.318), channel_id=1, source_target_pairs={{0,8},{8,16},{16,24},{24,32},{32,40},{40,48},{48,56},{56,64},{64,7... | collective-permute-start | bytes 196616 | tf_op jit(solution)/shard_map/while/body/eval_jaxpr/ppermute | solution.py:12
  220.4 13.2 %collective-permute-start.1 = (bf16[2,128,128]{2,1,0:T(8,128)(2,1)S(1)}, bf16[2,128,128]{2,1,0:T(8,128)(2,1)S(1)}, u32[]{:S(2)}, u32[]{:S(2)}) collective-permute-start(bf16[2,128,128]{2,1,0:T(8,128)(2,1)S(1)} %get-tuple-element.318), channel_id=1, source_target_pairs={{0,8},{8,16},{16,24},{24,32},{32,40},{40,48},{48,56},{56,64},{64,7... | collective-permute-start | bytes 196616 | tf_op jit(solution)/shard_map/while/body/eval_jaxpr/ppermute | solution.py:12
  261.8 13.2 %collective-permute-start.1 = (bf16[2,128,128]{2,1,0:T(8,128)(2,1)S(1)}, bf16[2,128,128]{2,1,0:T(8,128)(2,1)S(1)}, u32[]{:S(2)}, u32[]{:S(2)}) collective-permute-start(bf16[2,128,128]{2,1,0:T(8,128)(2,1)S(1)} %get-tuple-element.318), channel_id=1, source_target_pairs={{0,8},{8,16},{16,24},{24,32},{32,40},{40,48},{48,56},{56,64},{64,7... | collective-permute-start | bytes 196616 | tf_op jit(solution)/shard_map/while/body/eval_jaxpr/ppermute | solution.py:12
  275.6 13.2 %collective-permute-start.1 = (bf16[2,128,128]{2,1,0:T(8,128)(2,1)S(1)}, bf16[2,128,128]{2,1,0:T(8,128)(2,1)S(1)}, u32[]{:S(2)}, u32[]{:S(2)}) collective-permute-start(bf16[2,128,128]{2,1,0:T(8,128)(2,1)S(1)} %get-tuple-element.318), channel_id=1, source_target_pairs={{0,8},{8,16},{16,24},{24,32},{32,40},{40,48},{48,56},{56,64},{64,7... | collective-permute-start | bytes 196616 | tf_op jit(solution)/shard_map/while/body/eval_jaxpr/ppermute | solution.py:12
  317.1 13.2 %collective-permute-start.1 = (bf16[2,128,128]{2,1,0:T(8,128)(2,1)S(1)}, bf16[2,128,128]{2,1,0:T(8,128)(2,1)S(1)}, u32[]{:S(2)}, u32[]{:S(2)}) collective-permute-start(bf16[2,128,128]{2,1,0:T(8,128)(2,1)S(1)} %get-tuple-element.318), channel_id=1, source_target_pairs={{0,8},{8,16},{16,24},{24,32},{32,40},{40,48},{48,56},{56,64},{64,7... | collective-permute-start | bytes 196616 | tf_op jit(solution)/shard_map/while/body/eval_jaxpr/ppermute | solution.py:12
  358.5 13.2 %collective-permute-start.1 = (bf16[2,128,128]{2,1,0:T(8,128)(2,1)S(1)}, bf16[2,128,128]{2,1,0:T(8,128)(2,1)S(1)}, u32[]{:S(2)}, u32[]{:S(2)}) collective-permute-start(bf16[2,128,128]{2,1,0:T(8,128)(2,1)S(1)} %get-tuple-element.318), channel_id=1, source_target_pairs={{0,8},{8,16},{16,24},{24,32},{32,40},{40,48},{48,56},{56,64},{64,7... | collective-permute-start | bytes 196616 | tf_op jit(solution)/shard_map/while/body/eval_jaxpr/ppermute | solution.py:12
  399.9 13.2 %collective-permute-start.1 = (bf16[2,128,128]{2,1,0:T(8,128)(2,1)S(1)}, bf16[2,128,128]{2,1,0:T(8,128)(2,1)S(1)}, u32[]{:S(2)}, u32[]{:S(2)}) collective-permute-start(bf16[2,128,128]{2,1,0:T(8,128)(2,1)S(1)} %get-tuple-element.318), channel_id=1, source_target_pairs={{0,8},{8,16},{16,24},{24,32},{32,40},{40,48},{48,56},{56,64},{64,7... | collective-permute-start | bytes 196616 | tf_op jit(solution)/shard_map/while/body/eval_jaxpr/ppermute | solution.py:12
  441.4 13.2 %collective-permute-start.1 = (bf16[2,128,128]{2,1,0:T(8,128)(2,1)S(1)}, bf16[2,128,128]{2,1,0:T(8,128)(2,1)S(1)}, u32[]{:S(2)}, u32[]{:S(2)}) collective-permute-start(bf16[2,128,128]{2,1,0:T(8,128)(2,1)S(1)} %get-tuple-element.318), channel_id=1, source_target_pairs={{0,8},{8,16},{16,24},{24,32},{32,40},{40,48},{48,56},{56,64},{64,7... | collective-permute-start | bytes 196616 | tf_op jit(solution)/shard_map/while/body/eval_jaxpr/ppermute | solution.py:12
  482.8 13.2 %collective-permute-start.1 = (bf16[2,128,128]{2,1,0:T(8,128)(2,1)S(1)}, bf16[2,128,128]{2,1,0:T(8,128)(2,1)S(1)}, u32[]{:S(2)}, u32[]{:S(2)}) collective-permute-start(bf16[2,128,128]{2,1,0:T(8,128)(2,1)S(1)} %get-tuple-element.318), channel_id=1, source_target_pairs={{0,8},{8,16},{16,24},{24,32},{32,40},{40,48},{48,56},{56,64},{64,7... | collective-permute-start | bytes 196616 | tf_op jit(solution)/shard_map/while/body/eval_jaxpr/ppermute | solution.py:12
  524.2 13.2 %collective-permute-start.1 = (bf16[2,128,128]{2,1,0:T(8,128)(2,1)S(1)}, bf16[2,128,128]{2,1,0:T(8,128)(2,1)S(1)}, u32[]{:S(2)}, u32[]{:S(2)}) collective-permute-start(bf16[2,128,128]{2,1,0:T(8,128)(2,1)S(1)} %get-tuple-element.318), channel_id=1, source_target_pairs={{0,8},{8,16},{16,24},{24,32},{32,40},{40,48},{48,56},{56,64},{64,7... | collective-permute-start | bytes 196616 | tf_op jit(solution)/shard_map/while/body/eval_jaxpr/ppermute | solution.py:12
  538.0 13.2 %collective-permute-start.1 = (bf16[2,128,128]{2,1,0:T(8,128)(2,1)S(1)}, bf16[2,128,128]{2,1,0:T(8,128)(2,1)S(1)}, u32[]{:S(2)}, u32[]{:S(2)}) collective-permute-start(bf16[2,128,128]{2,1,0:T(8,128)(2,1)S(1)} %get-tuple-element.318), channel_id=1, source_target_pairs={{0,8},{8,16},{16,24},{24,32},{32,40},{40,48},{48,56},{56,64},{64,7... | collective-permute-start | bytes 196616 | tf_op jit(solution)/shard_map/while/body/eval_jaxpr/ppermute | solution.py:12
  579.5 13.2 %collective-permute-start.1 = (bf16[2,128,128]{2,1,0:T(8,128)(2,1)S(1)}, bf16[2,128,128]{2,1,0:T(8,128)(2,1)S(1)}, u32[]{:S(2)}, u32[]{:S(2)}) collective-permute-start(bf16[2,128,128]{2,1,0:T(8,128)(2,1)S(1)} %get-tuple-element.318), channel_id=1, source_target_pairs={{0,8},{8,16},{16,24},{24,32},{32,40},{40,48},{48,56},{56,64},{64,7... | collective-permute-start | bytes 196616 | tf_op jit(solution)/shard_map/while/body/eval_jaxpr/ppermute | solution.py:12
  620.9 13.2 %collective-permute-start.1 = (bf16[2,128,128]{2,1,0:T(8,128)(2,1)S(1)}, bf16[2,128,128]{2,1,0:T(8,128)(2,1)S(1)}, u32[]{:S(2)}, u32[]{:S(2)}) collective-permute-start(bf16[2,128,128]{2,1,0:T(8,128)(2,1)S(1)} %get-tuple-element.318), channel_id=1, source_target_pairs={{0,8},{8,16},{16,24},{24,32},{32,40},{40,48},{48,56},{56,64},{64,7... | collective-permute-start | bytes 196616 | tf_op jit(solution)/shard_map/while/body/eval_jaxpr/ppermute | solution.py:12
  662.3 13.2 %collective-permute-start.1 = (bf16[2,128,128]{2,1,0:T(8,128)(2,1)S(1)}, bf16[2,128,128]{2,1,0:T(8,128)(2,1)S(1)}, u32[]{:S(2)}, u32[]{:S(2)}) collective-permute-start(bf16[2,128,128]{2,1,0:T(8,128)(2,1)S(1)} %get-tuple-element.318), channel_id=1, source_target_pairs={{0,8},{8,16},{16,24},{24,32},{32,40},{40,48},{48,56},{56,64},{64,7... | collective-permute-start | bytes 196616 | tf_op jit(solution)/shard_map/while/body/eval_jaxpr/ppermute | solution.py:12
  703.7 13.2 %collective-permute-start.1 = (bf16[2,128,128]{2,1,0:T(8,128)(2,1)S(1)}, bf16[2,128,128]{2,1,0:T(8,128)(2,1)S(1)}, u32[]{:S(2)}, u32[]{:S(2)}) collective-permute-start(bf16[2,128,128]{2,1,0:T(8,128)(2,1)S(1)} %get-tuple-element.318), channel_id=1, source_target_pairs={{0,8},{8,16},{16,24},{24,32},{32,40},{40,48},{48,56},{56,64},{64,7... | collective-permute-start | bytes 196616 | tf_op jit(solution)/shard_map/while/body/eval_jaxpr/ppermute | solution.py:12
  745.2 13.2 %collective-permute-start.1 = (bf16[2,128,128]{2,1,0:T(8,128)(2,1)S(1)}, bf16[2,128,128]{2,1,0:T(8,128)(2,1)S(1)}, u32[]{:S(2)}, u32[]{:S(2)}) collective-permute-start(bf16[2,128,128]{2,1,0:T(8,128)(2,1)S(1)} %get-tuple-element.318), channel_id=1, source_target_pairs={{0,8},{8,16},{16,24},{24,32},{32,40},{40,48},{48,56},{56,64},{64,7... | collective-permute-start | bytes 196616 | tf_op jit(solution)/shard_map/while/body/eval_jaxpr/ppermute | solution.py:12
  786.6 13.2 %collective-permute-start.1 = (bf16[2,128,128]{2,1,0:T(8,128)(2,1)S(1)}, bf16[2,128,128]{2,1,0:T(8,128)(2,1)S(1)}, u32[]{:S(2)}, u32[]{:S(2)}) collective-permute-start(bf16[2,128,128]{2,1,0:T(8,128)(2,1)S(1)} %get-tuple-element.318), channel_id=1, source_target_pairs={{0,8},{8,16},{16,24},{24,32},{32,40},{40,48},{48,56},{56,64},{64,7... | collective-permute-start | bytes 196616 | tf_op jit(solution)/shard_map/while/body/eval_jaxpr/ppermute | solution.py:12
  800.4 13.2 %collective-permute-start.1 = (bf16[2,128,128]{2,1,0:T(8,128)(2,1)S(1)}, bf16[2,128,128]{2,1,0:T(8,128)(2,1)S(1)}, u32[]{:S(2)}, u32[]{:S(2)}) collective-permute-start(bf16[2,128,128]{2,1,0:T(8,128)(2,1)S(1)} %get-tuple-element.318), channel_id=1, source_target_pairs={{0,8},{8,16},{16,24},{24,32},{32,40},{40,48},{48,56},{56,64},{64,7... | collective-permute-start | bytes 196616 | tf_op jit(solution)/shard_map/while/body/eval_jaxpr/ppermute | solution.py:12
  841.8 13.2 %collective-permute-start.1 = (bf16[2,128,128]{2,1,0:T(8,128)(2,1)S(1)}, bf16[2,128,128]{2,1,0:T(8,128)(2,1)S(1)}, u32[]{:S(2)}, u32[]{:S(2)}) collective-permute-start(bf16[2,128,128]{2,1,0:T(8,128)(2,1)S(1)} %get-tuple-element.318), channel_id=1, source_target_pairs={{0,8},{8,16},{16,24},{24,32},{32,40},{40,48},{48,56},{56,64},{64,7... | collective-permute-start | bytes 196616 | tf_op jit(solution)/shard_map/while/body/eval_jaxpr/ppermute | solution.py:12
  883.3 13.2 %collective-permute-start.1 = (bf16[2,128,128]{2,1,0:T(8,128)(2,1)S(1)}, bf16[2,128,128]{2,1,0:T(8,128)(2,1)S(1)}, u32[]{:S(2)}, u32[]{:S(2)}) collective-permute-start(bf16[2,128,128]{2,1,0:T(8,128)(2,1)S(1)} %get-tuple-element.318), channel_id=1, source_target_pairs={{0,8},{8,16},{16,24},{24,32},{32,40},{40,48},{48,56},{56,64},{64,7... | collective-permute-start | bytes 196616 | tf_op jit(solution)/shard_map/while/body/eval_jaxpr/ppermute | solution.py:12
  924.7 13.2 %collective-permute-start.1 = (bf16[2,128,128]{2,1,0:T(8,128)(2,1)S(1)}, bf16[2,128,128]{2,1,0:T(8,128)(2,1)S(1)}, u32[]{:S(2)}, u32[]{:S(2)}) collective-permute-start(bf16[2,128,128]{2,1,0:T(8,128)(2,1)S(1)} %get-tuple-element.318), channel_id=1, source_target_pairs={{0,8},{8,16},{16,24},{24,32},{32,40},{40,48},{48,56},{56,64},{64,7... | collective-permute-start | bytes 196616 | tf_op jit(solution)/shard_map/while/body/eval_jaxpr/ppermute | solution.py:12
  966.1 13.2 %collective-permute-start.1 = (bf16[2,128,128]{2,1,0:T(8,128)(2,1)S(1)}, bf16[2,128,128]{2,1,0:T(8,128)(2,1)S(1)}, u32[]{:S(2)}, u32[]{:S(2)}) collective-permute-start(bf16[2,128,128]{2,1,0:T(8,128)(2,1)S(1)} %get-tuple-element.318), channel_id=1, source_target_pairs={{0,8},{8,16},{16,24},{24,32},{32,40},{40,48},{48,56},{56,64},{64,7... | collective-permute-start | bytes 196616 | tf_op jit(solution)/shard_map/while/body/eval_jaxpr/ppermute | solution.py:12
  (107 other events, 2915.3 us)
Sparse Core Ops, SparseCore 0:
  10.8 85.6 all-gather.1
